TPU v7x, 32 devices: a whole 2x2x4 slice. The times are simulated.
32 devices in a mesh: row: 8 (over y, x, core), col: 4 (over z).
Axes of the slice: x: 2, y: 2, z: 4, core: 2. Of those that a mesh axis runs over, the one named last changes fastest.
Arguments:
- queries: bfloat16 [512, 2, 2048], P('row', None, 'col'), may hold values from -15 to 15
- new_keys: bfloat16 [512, 2, 2048], P('row', None, 'col'), may hold values from -6 to 6
- new_values: bfloat16 [512, 2, 2048], P('row', None, 'col'), may hold values from -6 to 6
- cache_keys: bfloat16 [1024, 2, 2048], P('row', None, 'col'), may hold values from -6 to 6
- cache_values: bfloat16 [1024, 2, 2048], P('row', None, 'col'), may hold values from -6 to 6
- cached_len: int32 [2], replicated, may hold values from 256 to 1024, as said below
- residual: bfloat16 [512, 2, 2048], P('row'), may hold values from -4 to 4
- out_weight: bfloat16 [2048, 2048], P('col'), may hold values from -0.125 to 0.125
- norm_gain: float32 [2048], replicated, may hold values from 0.5 to 1.5
- expert_ids: int32 [512, 2, 6], P('row'), may hold values from 0 to 63, all different within a row; in each aligned block of 128 rows (0 to 127, 128 to 255, ..., all dimensions but the last counted through in order) at most 24 rows name the same one
- gate_values: float32 [512, 2, 6], P('row'), may hold values from 0.1 to 0.6
- w_gate: bfloat16 [256, 2048, 352], P(('row', 'col')), may hold values from -0.125 to 0.125
- w_up: bfloat16 [256, 2048, 352], P(('row', 'col')), may hold values from -0.125 to 0.125
- w_down: bfloat16 [256, 352, 2048], P(('row', 'col')), may hold values from -0.15625 to 0.15625
- shared_gate: bfloat16 [2048, 2816], P(None, 'col'), may hold values from -0.125 to 0.125
- shared_up: bfloat16 [2048, 2816], P(None, 'col'), may hold values from -0.125 to 0.125
- shared_down: bfloat16 [2816, 2048], P('col'), may hold values from -0.109375 to 0.109375
Outputs:
- mixed: bfloat16 [512, 2, 2048], P('row', None, 'col')
- ffn_out: bfloat16 [512, 2, 2048], P('row', None, 'col')
Inputs may be any that keep to these rules, and one draw needn't show every extreme that they name: `cached_len`: some request has exactly 1024 cached positions. `expert_ids`: each token names 6 different experts. Among the 128 tokens of one index of row (positions taken in order, requests inside), no expert is named more than 24 times, and in some such blocks one expert is named exactly 24 times.
All inputs are finite; a program needn't handle non-finite values.
Results may differ from a plain program's by a relative error of at most 0.023.
Values may be sent and summed in bfloat16 or wider, within the bound.
No kernel may reach another device: no remote copies, remote signals or barrier semaphores. Data moves between devices by JAX's collectives and lax.ppermute only.
A program may use at most 192 MiB of HBM per device.

v0:
```python
import math
import jax
import jax.numpy as jnp
from jax import lax
from jax.sharding import PartitionSpec as P

HD = 128
E = 64
TOPK = 6
GROUPS = 4
CAP = 24


def body(
    queries,
    new_keys,
    new_values,
    cache_keys,
    cache_values,
    cached_len,
    residual,
    out_weight,
    norm_gain,
    expert_ids,
    gate_values,
    w_gate,
    w_up,
    w_down,
    shared_gate,
    shared_up,
    shared_down,
):
    rows_here = queries.shape[0]
    requests = queries.shape[1]
    heads_here = queries.shape[2] // HD
    cache_rows = cache_keys.shape[0]
    block_rows = cache_rows + rows_here
    model_width = residual.shape[2]
    row_index = lax.axis_index("row")
    row_count = lax.axis_size("row")
    score_scale = 1.0 / math.sqrt(HD)
    keys_here = jnp.concatenate([cache_keys, new_keys], axis=0)
    values_here = jnp.concatenate([cache_values, new_values], axis=0)
    query_heads = queries.reshape(rows_here, requests, heads_here, HD)
    local_pos = row_index * rows_here + jnp.arange(rows_here, dtype=jnp.int32)
    key_piece = lax.all_gather(keys_here, "row", axis=0, tiled=True)
    key_count = key_piece.shape[0]
    global_row = jnp.arange(key_count, dtype=jnp.int32)
    shard_index = global_row // block_rows
    offset_rows = global_row % block_rows
    in_cache = offset_rows < cache_rows
    cache_pos = shard_index * cache_rows + offset_rows
    new_pos = shard_index * rows_here + offset_rows - cache_rows
    cache_ok = in_cache[None, :] & (cache_pos[None, :] < cached_len[:, None])
    new_ok = jnp.logical_not(in_cache)[None, :] & (new_pos[None, :] <= local_pos[:, None])
    allowed = cache_ok[:, None, None, :] | new_ok[None, None, :, :]
    key_heads = key_piece.reshape(key_count, requests, heads_here, HD)
    value_heads = lax.all_gather(values_here, "row", axis=0, tiled=True).reshape(
        key_count, requests, heads_here, HD
    )
    scores = (
        jnp.einsum("irhd,jrhd->rhij", query_heads, key_heads, preferred_element_type=jnp.float32)
        * score_scale
    )
    masked = jnp.where(allowed, scores, -1e30)
    old_max = jnp.full((requests, heads_here, rows_here), -1e30, jnp.float32)
    new_max = jnp.maximum(old_max, jnp.max(masked, axis=-1))
    weights_now = jnp.where(allowed, jnp.exp(masked - new_max[..., None]), 0.0)
    new_sum = jnp.sum(weights_now, axis=-1)
    product = jnp.einsum(
        "rhij,jrhd->rhid",
        weights_now.astype(jnp.bfloat16),
        value_heads,
        preferred_element_type=jnp.float32,
    )
    attended = (product / new_sum[..., None]).astype(jnp.bfloat16)
    head_weights = out_weight.reshape(heads_here, HD, model_width)
    attn_part = jnp.einsum(
        "rhid,hde->ire", attended, head_weights, preferred_element_type=jnp.float32
    )
    attn_full = lax.psum(attn_part.astype(jnp.bfloat16), "col").astype(jnp.float32)
    mixed_full = (residual.astype(jnp.float32) + attn_full).astype(jnp.bfloat16)
    mixed_f32 = mixed_full.astype(jnp.float32)
    normed = (
        mixed_f32
        * lax.rsqrt(jnp.mean(mixed_f32 * mixed_f32, axis=-1, keepdims=True) + 1e-06)
        * norm_gain
    ).astype(jnp.bfloat16)
    token_count = rows_here * requests
    tokens = normed.reshape(token_count, model_width)
    col_index = lax.axis_index("col")
    col_count = lax.axis_size("col")
    entries_here = w_gate.shape[0]
    experts_dev = max(1, entries_here // GROUPS)
    groups_dev = entries_here // experts_dev
    experts_per_row = col_count * entries_here // GROUPS
    slots = row_count * experts_dev * CAP
    chosen = expert_ids.reshape(token_count * TOPK)
    onehot = (chosen[:, None] == jnp.arange(E, dtype=jnp.int32)[None, :]).astype(jnp.int32)
    slot_index = jnp.sum(jnp.cumsum(onehot, axis=0) * onehot, axis=1) - 1
    dest_row = chosen // experts_per_row
    local_expert = chosen - (dest_row * col_count + col_index) * entries_here // GROUPS
    valid = (local_expert >= 0) & (local_expert < experts_dev)
    place = (dest_row * experts_dev + local_expert) * CAP + slot_index
    place = jnp.where(valid, place, -1).reshape(token_count, TOPK)
    hit = place[:, :, None] == jnp.arange(slots, dtype=jnp.int32)[None, None, :]
    dispatch = jnp.sum(hit.astype(jnp.float32), axis=1).astype(jnp.bfloat16)
    combine = jnp.sum(jnp.where(hit, gate_values.reshape(token_count, TOPK, 1), 0.0), axis=1)
    outgoing = lax.dot_general(
        dispatch, tokens, (((0,), (0,)), ((), ())), preferred_element_type=jnp.float32
    ).astype(jnp.bfloat16)
    outgoing = outgoing.reshape(row_count, experts_dev, CAP, model_width)
    arrived = lax.all_to_all(outgoing, "row", 0, 0, tiled=True)
    hidden = w_gate.shape[2]
    wg = w_gate.reshape(experts_dev, groups_dev, model_width, hidden)
    wu = w_up.reshape(experts_dev, groups_dev, model_width, hidden)
    wd = w_down.reshape(experts_dev, groups_dev, hidden, model_width)
    gate_proj = jnp.einsum("nlsd,lgdf->lgnsf", arrived, wg, preferred_element_type=jnp.float32)
    up_proj = jnp.einsum("nlsd,lgdf->lgnsf", arrived, wu, preferred_element_type=jnp.float32)
    hidden_act = (jax.nn.silu(gate_proj) * up_proj).astype(jnp.bfloat16)
    expert_out = jnp.einsum(
        "lgnsf,lgfd->nlsd", hidden_act, wd, preferred_element_type=jnp.float32
    ).astype(jnp.bfloat16)
    returned = lax.all_to_all(expert_out, "row", 0, 0, tiled=True).reshape(slots, model_width)
    combine_hi = combine.astype(jnp.bfloat16)
    combine_lo = (combine - combine_hi.astype(jnp.float32)).astype(jnp.bfloat16)
    routed = jnp.dot(combine_hi, returned, preferred_element_type=jnp.float32) + jnp.dot(
        combine_lo, returned, preferred_element_type=jnp.float32
    )
    shared_g = jnp.dot(tokens, shared_gate, preferred_element_type=jnp.float32)
    shared_u = jnp.dot(tokens, shared_up, preferred_element_type=jnp.float32)
    shared_act = (jax.nn.silu(shared_g) * shared_u).astype(jnp.bfloat16)
    shared_part = jnp.dot(shared_act, shared_down, preferred_element_type=jnp.float32)
    ffn_total = lax.psum_scatter(
        (routed + shared_part).astype(jnp.bfloat16), "col", scatter_dimension=1, tiled=True
    )
    col_width = model_width // col_count
    ffn_here = ffn_total.reshape(rows_here, requests, col_width)
    mixed_here = lax.dynamic_slice_in_dim(mixed_full, col_index * col_width, col_width, 2)
    return (mixed_here, ffn_here)


def solution(mesh):
    in_specs = (
        P("row", None, "col"),
        P("row", None, "col"),
        P("row", None, "col"),
        P("row", None, "col"),
        P("row", None, "col"),
        P(),
        P("row", None, None),
        P("col", None),
        P(),
        P("row", None, None),
        P("row", None, None),
        P(("row", "col"), None, None),
        P(("row", "col"), None, None),
        P(("row", "col"), None, None),
        P(None, "col"),
        P(None, "col"),
        P("col", None),
    )
    out_specs = (P("row", None, "col"), P("row", None, "col"))
    return jax.shard_map(body, mesh=mesh, in_specs=in_specs, out_specs=out_specs, check_vma=False)
```

profile of v0, /device:TPU:0, one launch (start us, length us, event | category | flops | bytes accessed | tf_op | source)
XLA Modules:
  0.0 250.1 jit_solution(14127599166133961431)
XLA Ops:
  7.2 2.4 pad_maximum_fusion
  9.8 2.3 pad_maximum_fusion.1
  12.1 0.8 copy.73
  13.2 1.0 reshape.257
  14.2 1.8 reduce-window.6
  16.9 28.1 %all-gather.3.cloned.1.call-done = bf16[1536,2,512]{2,1,0:T(2,128)(2,1)} async-done(((bf16[192,2,512]{2,1,0:T(2,128)(2,1)}), bf16[1536,2,512]{2,1,0:T(2,128)(2,1)}) %all-gather.3.cloned.1.call-update) | async-done | bytes 3145744 | tf_op jit(solution)/shard_map/all_gather | solution.py:46
  45.0 8.7 %copy.68 = bf16[1536,2,512]{0,2,1:T(8,128)(2,1)} copy(bf16[1536,2,512]{2,1,0:T(2,128)(2,1)} %all-gather.3.cloned.1.call-done) | data formatting | bytes 6291456 | tf_op jit(solution)/shard_map/all_gather | solution.py:46
  53.7 3.0 %fusion.62 = (f32[2,4,64]{2,1,0:T(4,128)S(1)}, f32[2,4,64,1536]{3,2,1,0:T(8,128)S(1)}) fusion(bf16[1536,2,4,128]{0,3,2,1:T(8,128)(2,1)} %bitcast.114, bf16[64,2,4,128]{3,2,1,0:T(4,128)(2,1)S(1)} %reshape.257, pred[2,64,1536]{2,1,0:T(8,128)(4,1)S(1)} %broadcast_or_fusion), kind=kOutput, calls=%fused_computation.106 | convolution fusion | flops 203685376 | bytes 6621184 | tf_op jit(solution)/shard_map/irhd,jrhd->rhij/dot_general | solution.py:62
  56.7 1.7 copy-done.1
  58.4 0.8 fusion.3
  59.2 20.0 %all-gather.5.cloned.1.call-done = bf16[1536,2,512]{2,1,0:T(2,128)(2,1)} async-done(((bf16[192,2,512]{2,1,0:T(2,128)(2,1)}), bf16[1536,2,512]{2,1,0:T(2,128)(2,1)}) %all-gather.5.cloned.1.call-update) | async-done | bytes 3145744 | tf_op jit(solution)/shard_map/all_gather | solution.py:58
  79.2 8.7 %copy.71 = bf16[1536,2,512]{0,2,1:T(8,128)(2,1)} copy(bf16[1536,2,512]{2,1,0:T(2,128)(2,1)} %all-gather.5.cloned.1.call-done) | data formatting | bytes 6291456 | tf_op jit(solution)/shard_map/all_gather | solution.py:58
  87.9 5.9 %fusion.11 = bf16[64,2,2048]{2,0,1:T(8,128)(2,1)} fusion(bf16[4,128,2048,1]{2,1,0,3:T(8,128)(2,1)} %bitcast.123, bf16[1536,2,4,128]{0,3,2,1:T(8,128)(2,1)} %bitcast.116, f32[2,4,64,1536]{3,2,1,0:T(8,128)} %copy-done.1, f32[2,4,64]{2,1,0:T(4,128)S(1)} %broadcast_maximum_fusion, pred[2,64,1536]{2,1,0:T(8,128)(4,1)S(1)} %broadcast_or_fusion, ...), kind=kOutput, calls=%fused_computation.21 | convolution fusion | flops 472514560 | bytes 9113600 | tf_op jit(solution)/shard_map/rhid,hde->ire/dot_general | solution.py:78
  94.3 1.0 select_reduce_fusion
  95.3 37.0 %all-reduce.2.cloned.1.call-done = bf16[64,2,2048]{2,0,1:T(8,128)(2,1)} async-done(((bf16[64,2,2048]{2,0,1:T(8,128)(2,1)}), bf16[64,2,2048]{2,0,1:T(8,128)(2,1)}) %all-reduce.2.cloned.1.call-update) | async-done | bytes 524304 | tf_op jit(solution)/shard_map/psum | solution.py:81
  132.3 1.5 fusion.29
  133.8 0.8 copy-done.2
  134.8 1.3 copy.80
  136.2 1.2 reshape.262
  138.0 24.4 %all_to_all.10 = bf16[8,2,24,2048]{3,2,1,0:T(8,128)(2,1)S(1)} all-to-all(bf16[8,2,24,2048]{3,2,1,0:T(8,128)(2,1)S(1)} %bitcast.115), channel_id=1, replica_groups=mesh['row'=8,'col'=4] {'row'}, dimensions={0} | all-to-all | bytes 3145728 | tf_op jit(solution)/shard_map/all_to_all | solution.py:113
  162.4 8.5 %fusion.17 = f32[2,8,24,4,352]{4,2,3,1,0:T(8,128)} fusion(bf16[2,4,2048,352,1]{2,3,1,4,0:T(8,128)(2,1)} %bitcast.120, bf16[8,2,24,2048]{3,2,1,0:T(8,128)(2,1)S(1)} %all_to_all.10), kind=kOutput, calls=%fused_computation.26 | convolution fusion | flops 2214592512 | bytes 15269888 | tf_op jit(solution)/shard_map/nlsd,lgdf->lgnsf/dot_general | solution.py:119
  171.0 12.9 %fusion.2 = bf16[8,2,24,2048]{3,2,0,1:T(8,128)(2,1)} fusion(bf16[2,4,352,2048,1]{3,2,1,4,0:T(8,128)(2,1)} %bitcast.121, f32[2,8,24,4,352]{4,2,3,1,0:T(8,128)} %fusion.17, bf16[2,4,2048,352,1]{2,3,1,4,0:T(8,128)(2,1)} %bitcast.122, bf16[8,2,24,2048]{3,2,1,0:T(8,128)(2,1)} %copy-done.4), kind=kOutput, calls=%fused_computation.6 | convolution fusion | flops 4433215488 | bytes 28377088 | tf_op jit(solution)/shard_map/lgnsf,lgfd->nlsd/dot_general | solution.py:121
  183.9 2.7 %copy.83 = bf16[8,2,24,2048]{3,2,1,0:T(8,128)(2,1)} copy(bf16[8,2,24,2048]{3,2,0,1:T(8,128)(2,1)} %fusion.2) | data formatting | bytes 3145728 | tf_op jit(solution)/shard_map/convert_element_type | solution.py:123
  186.6 4.3 %all-to-all-start.1 = ((bf16[8,2,24,2048]{3,2,1,0:T(8,128)(2,1)}), bf16[8,2,24,2048]{3,2,1,0:T(8,128)(2,1)}, u32[]{:S(2)}, u32[]{:S(2)}) async-start(bf16[8,2,24,2048]{3,2,1,0:T(8,128)(2,1)} %copy.83), calls=%async_computation.1 | async-start | bytes 3145728 | tf_op jit(solution)/shard_map/all_to_all | solution.py:124
  191.0 3.5 %fusion.63 = f32[128,704]{0,1:T(8,128)} fusion(bf16[128,2048]{1,0:T(8,128)(2,1)S(1)} %reshape.262, bf16[2048,704]{0,1:T(8,128)(2,1)} %param.31), kind=kOutput, calls=%fused_computation.107 | convolution fusion | flops 369098752 | bytes 3768320 | tf_op jit(solution)/shard_map/dot_general | solution.py:130
  194.4 17.5 %all-to-all-done.1 = bf16[8,2,24,2048]{3,2,1,0:T(8,128)(2,1)} async-done(((bf16[8,2,24,2048]{3,2,1,0:T(8,128)(2,1)}), bf16[8,2,24,2048]{3,2,1,0:T(8,128)(2,1)}, u32[]{:S(2)}, u32[]{:S(2)}) %all-to-all-start.1) | async-done | bytes 1572896 | tf_op jit(solution)/shard_map/all_to_all | solution.py:124
  212.0 2.0 fusion.50
  214.0 2.8 %convolution_add_fusion.1 = f32[128,2048]{1,0:T(8,128)} fusion(f32[128,2048]{1,0:T(8,128)S(1)} %fusion.50, bf16[384,2048]{1,0:T(8,128)(2,1)} %bitcast.28, f32[128,384]{1,0:T(8,128)S(1)} %copy-done.3), kind=kOutput, calls=%fused_computation.10 | convolution fusion | flops 201785344 | bytes 3866624 | tf_op jit(solution)/shard_map/dot_general | solution.py:127
  216.8 5.1 %fusion.5 = bf16[128,2048]{1,0:T(8,128)(2,1)} fusion(f32[128,2048]{1,0:T(8,128)} %convolution_add_fusion.1, bf16[704,2048]{1,0:T(8,128)(2,1)S(1)} %copy-done, bf16[128,2048]{1,0:T(8,128)(2,1)S(1)} %reshape.262, bf16[2048,704]{0,1:T(8,128)(2,1)} %param.32, f32[128,704]{0,1:T(8,128)} %fusion.63), kind=kOutput, calls=%fused_computation.12 | convolution fusion | flops 739262464 | bytes 8224768 | tf_op jit(solution)/shard_map/dot_general | solution.py:133
  221.9 0.9 constant_dynamic-slice_fusion
  223.7 18.3 %reduce-scatter.2.cloned.1.call-done = bf16[128,512]{1,0:T(8,128)(2,1)} async-done(((bf16[128,2048]{1,0:T(8,128)(2,1)}), bf16[128,512]{1,0:T(8,128)(2,1)}) %reduce-scatter.2.cloned.1.call-update) | async-done | bytes 131088 | tf_op jit(solution)/shard_map/reduce_scatter | solution.py:134
  241.9 1.6 reshape.268
  (47 shorter events, 3.4 us)
Async XLA Ops:
  7.2 209.6 %copy-start = (bf16[704,2048]{1,0:T(8,128)(2,1)S(1)}, bf16[704,2048]{1,0:T(8,128)(2,1)}, u32[]{:S(2)}) copy-start(bf16[704,2048]{1,0:T(8,128)(2,1)} %param.33) | copy-start | bytes 8650756
  7.2 9.4 %copy-start.7 = (s32[2]{0:T(128)S(1)}, s32[2]{0:T(128)}, u32[]{:S(2)}) copy-start(s32[2]{0:T(128)} %param.22) | copy-start | bytes 28
  7.2 37.8 %all-gather.3.cloned.1.call-start = ((), (), s32[]{:S(2)}) async-start(), calls=%async_computation.3 | async-start | bytes 3538944 | tf_op jit(solution)/shard_map/all_gather | solution.py:46
  9.7 69.5 %all-gather.5.cloned.1.call-start = ((), (), s32[]{:S(2)}) async-start(), calls=%async_computation.4 | async-start | bytes 3538944 | tf_op jit(solution)/shard_map/all_gather | solution.py:58
  12.1 120.3 %all-reduce.2.cloned.1.call-start = ((), (), s32[]{:S(2)}) async-start(), calls=%async_computation.5 | async-start | bytes 1048576 | tf_op jit(solution)/shard_map/psum | solution.py:81
  56.7 1.7 copy-start.1
  87.9 6.3 %copy-start.6 = (f32[64,2,6]{0,1,2:T(2,128)S(1)}, f32[64,2,6]{0,1,2:T(2,128)}, u32[]{:S(2)}) copy-start(f32[64,2,6]{0,1,2:T(2,128)} %param.27) | copy-start | bytes 9220
  93.8 40.9 %copy-start.5 = (f32[2048]{0:T(1024)S(1)}, f32[2048]{0:T(1024)}, u32[]{:S(2)}) copy-start(f32[2048]{0:T(1024)} %param.25) | copy-start | bytes 24580
  133.8 0.8 copy-start.2
  162.4 8.5 %copy-start.4 = (bf16[8,2,24,2048]{3,2,1,0:T(8,128)(2,1)}, bf16[8,2,24,2048]{3,2,1,0:T(8,128)(2,1)S(1)}, u32[]{:S(2)}) copy-start(bf16[8,2,24,2048]{3,2,1,0:T(8,128)(2,1)S(1)} %all_to_all.10) | copy-start | bytes 4718596
  186.6 25.3 %all-to-all-start.1 = ((bf16[8,2,24,2048]{3,2,1,0:T(8,128)(2,1)}), bf16[8,2,24,2048]{3,2,1,0:T(8,128)(2,1)}, u32[]{:S(2)}, u32[]{:S(2)}) async-start(bf16[8,2,24,2048]{3,2,1,0:T(8,128)(2,1)} %copy.83), calls=%async_computation.1 | async-start | bytes 3145728 | tf_op jit(solution)/shard_map/all_to_all | solution.py:124
  190.9 51.0 %reduce-scatter.2.cloned.1.call-start = ((), (), s32[]{:S(2)}) async-start(), calls=%async_computation.6 | async-start | bytes 655360 | tf_op jit(solution)/shard_map/reduce_scatter | solution.py:134
  212.0 2.0 copy-start.3
Sparse Core Ops, SparseCore 0:
  9.9 35.0 all-gather.2
  46.8 32.3 all-gather.4
  93.9 38.3 all-reduce.1
  222.1 19.8 reduce-scatter.1
where the time goes:
time: 251 us; the launch traced here: 250 us
  waiting for transfers between devices  121 us (48%)
  matrix products  44.3 us (18%)
  local copies, waits for them, and re-layouts  31.3 us (12%)
  blocking collectives  24.4 us (10%)
  between operations  14 us (6%)
  other arithmetic  10.7 us (4%)
  starting transfers between devices  4.45 us (2%)
    psum x1, waiting for transfers between devices, body(): lax.psum(attn_part.astype(jnp.bfloat16), 'col').astype(jnp.float32)  37 us
    all_gather x1, waiting for transfers between devices, body(): key_piece = lax.all_gather(keys_here, 'row', axis=0, tiled=True)  28.1 us
    all_to_all x1, blocking collectives, body(): arrived = lax.all_to_all(outgoing, 'row', 0, 0, tiled=True)  24.4 us
    all_gather x1, waiting for transfers between devices, body(): lax.all_gather(values_here, 'row', axis=0, tiled=True)  20 us
    reduce_scatter x1, waiting for transfers between devices, body(): lax.psum_scatter((routed + shared_part).astype(jnp.bfloat16), 'col', scat...  18.3 us
    all_to_all x1, waiting for transfers between devices, body(): lax.all_to_all(expert_out, 'row', 0, 0, tiled=True)  17.5 us
    dot_general x1, matrix products, body(): jnp.einsum('lgnsf,lgfd->nlsd', hidden_act, wd, preferred_element_type=jnp...  12.9 us
    all_gather x1, local copies, waits for them, and re-layouts, body(): key_piece = lax.all_gather(keys_here, 'row', axis=0, tiled=True)  8.71 us
  transfers between devices with their start and end apart: 5, of which 5 were waited for; matrix products, arithmetic and copies ran while one was open for 10% of the time, Pallas kernels for 0%

commit v1 on v0

--- a/solution.py
+++ b/solution.py
@@ -3,12 +3,29 @@
 import jax.numpy as jnp
 from jax import lax
 from jax.sharding import PartitionSpec as P
+from jax.lax import axis_index, axis_size, ppermute
 
 HD = 128
 E = 64
 TOPK = 6
 GROUPS = 4
 CAP = 24
+
+
+def _pass_roads(mine, axis_key="row"):
+    shelf = []
+    num = axis_size(axis_key)
+    for nth in tuple(range(1, num)):
+        shelf.append((nth - 1, nth))
+    known = mine
+    grid = [known]
+    shaped = shelf + [(num - 1, 0)]
+    for _ in [*range(num - 1)]:
+        known = ppermute(known, axis_key, shaped)
+        grid += [known]
+    block_out = jnp.concatenate([*reversed(grid)], axis=0)
+    clean = jnp.roll(block_out, (axis_index(axis_key) + 1) * known.shape[0], axis=0)
+    return clean
 
 
 def body(
@@ -43,7 +60,7 @@
     values_here = jnp.concatenate([cache_values, new_values], axis=0)
     query_heads = queries.reshape(rows_here, requests, heads_here, HD)
     local_pos = row_index * rows_here + jnp.arange(rows_here, dtype=jnp.int32)
-    key_piece = lax.all_gather(keys_here, "row", axis=0, tiled=True)
+    key_piece = _pass_roads(keys_here)
     key_count = key_piece.shape[0]
     global_row = jnp.arange(key_count, dtype=jnp.int32)
     shard_index = global_row // block_rows

time: 251 us -> 282 us (1.12)
  waiting for transfers between devices: 121 us -> 138 us
  local copies, waits for them, and re-layouts: 31.3 us -> 42.7 us
    ppermute x0 -> x7, waiting for transfers between devices: none -> 65.9 us  [_pass_roads(): known = ppermute(known, axis_key, shaped)]
    all_gather x1 -> x0, waiting for transfers between devices: 28.1 us -> none  [body(): key_piece = lax.all_gather(keys_here, 'row', axis=0, tiled=True)]
    all_gather x1, waiting for transfers between devices: 20 us -> 0.01 us  [body(): lax.all_gather(values_here, 'row', axis=0, tiled=True)]
    concatenate x0 -> x1, local copies, waits for them, and re-layouts: none -> 11.8 us  [_pass_roads(): jnp.roll(block_out, (axis_index(axis_key) + 1) * known.shape[0], axis=0)]
    all_gather x1 -> x0, local copies, waits for them, and re-layouts: 8.71 us -> none  [body(): key_piece = lax.all_gather(keys_here, 'row', axis=0, tiled=True)]
    dynamic_slice x0 -> x1, local copies, waits for them, and re-layouts: none -> 3.54 us  [_pass_roads(): jnp.roll(block_out, (axis_index(axis_key) + 1) * known.shape[0], axis=0)]
    unnamed x19 -> x31, local copies, waits for them, and re-layouts: 4.27 us -> 7.43 us
  transfers between devices with their start and end apart: 5 -> 11, of which waited for: 5 -> 10; matrix products, arithmetic and copies ran while one was open for 10% -> 13% of each run, Pallas kernels for 0% -> 0%
where the time goes in v1:
time: 282 us; the launch traced here: 280 us
  waiting for transfers between devices  138 us (49%)
  local copies, waits for them, and re-layouts  42.7 us (15%)
  matrix products  42.3 us (15%)
  blocking collectives  24.4 us (9%)
  between operations  14 us (5%)
  other arithmetic  13.4 us (5%)
  starting transfers between devices  4.92 us (2%)
    ppermute x7, waiting for transfers between devices, _pass_roads(): known = ppermute(known, axis_key, shaped)  65.9 us
    psum x1, waiting for transfers between devices, body(): lax.psum(attn_part.astype(jnp.bfloat16), 'col').astype(jnp.float32)  36.1 us
    all_to_all x1, blocking collectives, body(): arrived = lax.all_to_all(outgoing, 'row', 0, 0, tiled=True)  24.4 us
    reduce_scatter x1, waiting for transfers between devices, body(): lax.psum_scatter((routed + shared_part).astype(jnp.bfloat16), 'col', scat...  18.3 us
    all_to_all x1, waiting for transfers between devices, body(): lax.all_to_all(expert_out, 'row', 0, 0, tiled=True)  17.5 us
    dot_general x1, matrix products, body(): jnp.einsum('lgnsf,lgfd->nlsd', hidden_act, wd, preferred_element_type=jnp...  12.9 us
    concatenate x1, local copies, waits for them, and re-layouts, _pass_roads(): jnp.roll(block_out, (axis_index(axis_key) + 1) * known.shape[0], axis=0)  11.8 us
    all_gather x1, local copies, waits for them, and re-layouts, body(): lax.all_gather(values_here, 'row', axis=0, tiled=True)  8.72 us
  transfers between devices with their start and end apart: 11, of which 10 were waited for; matrix products, arithmetic and copies ran while one was open for 13% of the time, Pallas kernels for 0%

profile of v1, /device:TPU:0, one launch (start us, length us, event | category | flops | bytes accessed | tf_op | source)
XLA Modules:
  0.0 279.6 jit_solution(1688120642853457349)
XLA Ops:
  7.2 2.5 pad_maximum_fusion.1
  12.7 9.9 %collective-permute-done = bf16[192,2,512]{0,2,1:T(8,128)(2,1)} collective-permute-done((bf16[192,2,512]{0,2,1:T(8,128)(2,1)S(1)}, bf16[192,2,512]{0,2,1:T(8,128)(2,1)}, u32[]{:S(2)}, u32[]{:S(2)}) %collective-permute-start) | collective-permute-done | bytes 393248 | tf_op jit(solution)/shard_map/ppermute | solution.py:24
  22.8 10.9 %collective-permute-done.1 = bf16[192,2,512]{0,2,1:T(8,128)(2,1)} collective-permute-done((bf16[192,2,512]{0,2,1:T(8,128)(2,1)}, bf16[192,2,512]{0,2,1:T(8,128)(2,1)}, u32[]{:S(2)}, u32[]{:S(2)}) %collective-permute-start.1) | collective-permute-done | bytes 393248 | tf_op jit(solution)/shard_map/ppermute | solution.py:24
  34.3 4.4 %reduce-window.6 = s32[64,6,128]{2,0,1:T(8,128)} reduce-window(s32[64,6,128]{2,0,1:T(8,128)} %fusion.39, s32[]{:T(128)} %constant.91.clone.1), window={size=1x1x128 pad=0_0x0_0x127_0}, to_apply=%region_3.4 | reduce-window | flops 6242304 | bytes 393220 | tf_op jit(solution)/shard_map/reduce-window
  38.8 1.2 slice_reduce_fusion
  40.0 10.5 %collective-permute-done.2 = bf16[192,2,512]{0,2,1:T(8,128)(2,1)} collective-permute-done((bf16[192,2,512]{0,2,1:T(8,128)(2,1)}, bf16[192,2,512]{0,2,1:T(8,128)(2,1)}, u32[]{:S(2)}, u32[]{:S(2)}) %collective-permute-start.2) | collective-permute-done | bytes 393248 | tf_op jit(solution)/shard_map/ppermute | solution.py:24
  50.6 1.6 reshape.257
  53.4 6.9 %collective-permute-done.3 = bf16[192,2,512]{0,2,1:T(8,128)(2,1)} collective-permute-done((bf16[192,2,512]{0,2,1:T(8,128)(2,1)}, bf16[192,2,512]{0,2,1:T(8,128)(2,1)}, u32[]{:S(2)}, u32[]{:S(2)}) %collective-permute-start.3) | collective-permute-done | bytes 393248 | tf_op jit(solution)/shard_map/ppermute | solution.py:24
  60.4 9.6 %collective-permute-done.4 = bf16[192,2,512]{0,2,1:T(8,128)(2,1)S(1)} collective-permute-done((bf16[192,2,512]{0,2,1:T(8,128)(2,1)}, bf16[192,2,512]{0,2,1:T(8,128)(2,1)S(1)}, u32[]{:S(2)}, u32[]{:S(2)}) %collective-permute-start.4) | collective-permute-done | bytes 393248 | tf_op jit(solution)/shard_map/ppermute | solution.py:24
  70.9 9.4 %collective-permute-done.5 = bf16[192,2,512]{0,2,1:T(8,128)(2,1)S(1)} collective-permute-done((bf16[192,2,512]{0,2,1:T(8,128)(2,1)S(1)}, bf16[192,2,512]{0,2,1:T(8,128)(2,1)S(1)}, u32[]{:S(2)}, u32[]{:S(2)}) %collective-permute-start.5) | collective-permute-done | bytes 393248 | tf_op jit(solution)/shard_map/ppermute | solution.py:24
  81.9 8.8 %collective-permute-done.6 = bf16[192,2,512]{0,2,1:T(8,128)(2,1)} collective-permute-done((bf16[192,2,512]{0,2,1:T(8,128)(2,1)S(1)}, bf16[192,2,512]{0,2,1:T(8,128)(2,1)}, u32[]{:S(2)}, u32[]{:S(2)}) %collective-permute-start.6) | collective-permute-done | bytes 393248 | tf_op jit(solution)/shard_map/ppermute | solution.py:24
  90.8 11.8 %concatenate.14 = bf16[3072,2,512]{0,2,1:T(8,128)(2,1)} concatenate(bf16[192,2,512]{0,2,1:T(8,128)(2,1)} %collective-permute-done.6, bf16[192,2,512]{0,2,1:T(8,128)(2,1)} %copy-done.4, bf16[192,2,512]{0,2,1:T(8,128)(2,1)} %copy-done.3, bf16[192,2,512]{0,2,1:T(8,128)(2,1)} %collective-permute-done.3, bf16[192,2,512]{0,2,1:T(8,128)(2,1)} %collective-permute-done.2, ...), dimensions={0} | concatenate | bytes 12582912 | tf_op jit(solution)/shard_map/jit(_roll_dynamic)/concatenate | solution.py:27
  102.6 3.5 %constant_dynamic-slice_fusion.1 = bf16[1536,2,512]{0,2,1:T(8,128)(2,1)S(1)} fusion(bf16[3072,2,512]{0,2,1:T(8,128)(2,1)} %concatenate.14, s32[]{:T(128)S(6)} %select_n.93), kind=kLoop, calls=%fused_computation.104 | loop fusion | bytes 6291460 | tf_op jit(solution)/shard_map/jit(_roll_dynamic)/dynamic_slice | solution.py:27
  107.2 1.6 copy-done.1
  109.7 8.7 %copy.90 = bf16[1536,2,512]{0,2,1:T(8,128)(2,1)} copy(bf16[1536,2,512]{2,1,0:T(2,128)(2,1)} %all-gather.2.cloned.1.call-done) | data formatting | bytes 6291456 | tf_op jit(solution)/shard_map/all_gather | solution.py:75
  118.4 5.9 %fusion.11 = bf16[64,2,2048]{2,0,1:T(8,128)(2,1)} fusion(bf16[4,128,2048,1]{2,1,0,3:T(8,128)(2,1)} %bitcast.123, bf16[1536,2,4,128]{0,3,2,1:T(8,128)(2,1)} %bitcast.116, f32[2,4,64,1536]{3,2,1,0:T(8,128)} %copy-done.1, f32[2,4,64]{2,1,0:T(4,128)S(1)} %broadcast_maximum_fusion, pred[2,64,1536]{2,1,0:T(8,128)(4,1)S(1)} %copy-done.5, f32[2,4,64]{2,1,0:T(4,128)S(1)} %fusion.3), kind=kOutput, calls=%fused_computation.21 | convolution fusion | flops 472514560 | bytes 9113600 | tf_op jit(solution)/shard_map/rhid,hde->ire/dot_general | solution.py:95
  125.8 36.1 %all-reduce.2.cloned.1.call-done = bf16[64,2,2048]{2,0,1:T(8,128)(2,1)} async-done(((bf16[64,2,2048]{2,0,1:T(8,128)(2,1)}), bf16[64,2,2048]{2,0,1:T(8,128)(2,1)}) %all-reduce.2.cloned.1.call-update) | async-done | bytes 524304 | tf_op jit(solution)/shard_map/psum | solution.py:98
  161.9 1.5 fusion.29
  164.4 1.3 copy.99
  165.8 1.2 reshape.262
  167.6 24.4 %all_to_all.10 = bf16[8,2,24,2048]{3,2,1,0:T(8,128)(2,1)S(1)} all-to-all(bf16[8,2,24,2048]{3,2,1,0:T(8,128)(2,1)S(1)} %bitcast.115), channel_id=1, replica_groups=mesh['row'=8,'col'=4] {'row'}, dimensions={0} | all-to-all | bytes 3145728 | tf_op jit(solution)/shard_map/all_to_all | solution.py:130
  192.0 8.5 %fusion.17 = f32[2,8,24,4,352]{4,2,3,1,0:T(8,128)} fusion(bf16[2,4,2048,352,1]{2,3,1,4,0:T(8,128)(2,1)} %bitcast.120, bf16[8,2,24,2048]{3,2,1,0:T(8,128)(2,1)S(1)} %all_to_all.10), kind=kOutput, calls=%fused_computation.26 | convolution fusion | flops 2214592512 | bytes 15269888 | tf_op jit(solution)/shard_map/nlsd,lgdf->lgnsf/dot_general | solution.py:136
  200.6 12.9 %fusion.2 = bf16[8,2,24,2048]{3,2,0,1:T(8,128)(2,1)} fusion(bf16[2,4,352,2048,1]{3,2,1,4,0:T(8,128)(2,1)} %bitcast.121, f32[2,8,24,4,352]{4,2,3,1,0:T(8,128)} %fusion.17, bf16[2,4,2048,352,1]{2,3,1,4,0:T(8,128)(2,1)} %bitcast.122, bf16[8,2,24,2048]{3,2,1,0:T(8,128)(2,1)} %copy-done.7), kind=kOutput, calls=%fused_computation.6 | convolution fusion | flops 4433215488 | bytes 28377088 | tf_op jit(solution)/shard_map/lgnsf,lgfd->nlsd/dot_general | solution.py:138
  213.5 2.7 copy.102
  216.2 4.3 %all-to-all-start.1 = ((bf16[8,2,24,2048]{3,2,1,0:T(8,128)(2,1)}), bf16[8,2,24,2048]{3,2,1,0:T(8,128)(2,1)}, u32[]{:S(2)}, u32[]{:S(2)}) async-start(bf16[8,2,24,2048]{3,2,1,0:T(8,128)(2,1)} %copy.102), calls=%async_computation.1 | async-start | bytes 3145728 | tf_op jit(solution)/shard_map/all_to_all | solution.py:141
  220.5 3.5 %fusion.63 = f32[128,704]{0,1:T(8,128)} fusion(bf16[128,2048]{1,0:T(8,128)(2,1)S(1)} %reshape.262, bf16[2048,704]{0,1:T(8,128)(2,1)} %param.31), kind=kOutput, calls=%fused_computation.108 | convolution fusion | flops 369098752 | bytes 3768320 | tf_op jit(solution)/shard_map/dot_general | solution.py:147
  224.0 17.5 %all-to-all-done.1 = bf16[8,2,24,2048]{3,2,1,0:T(8,128)(2,1)} async-done(((bf16[8,2,24,2048]{3,2,1,0:T(8,128)(2,1)}), bf16[8,2,24,2048]{3,2,1,0:T(8,128)(2,1)}, u32[]{:S(2)}, u32[]{:S(2)}) %all-to-all-start.1) | async-done | bytes 1572896 | tf_op jit(solution)/shard_map/all_to_all | solution.py:141
  241.5 2.0 fusion.50
  243.5 2.8 %convolution_add_fusion.1 = f32[128,2048]{1,0:T(8,128)} fusion(f32[128,2048]{1,0:T(8,128)S(1)} %fusion.50, bf16[384,2048]{1,0:T(8,128)(2,1)} %bitcast.28, f32[128,384]{1,0:T(8,128)S(1)} %copy-done.6), kind=kOutput, calls=%fused_computation.10 | convolution fusion | flops 201785344 | bytes 3866624 | tf_op jit(solution)/shard_map/dot_general | solution.py:144
  246.3 5.1 %fusion.5 = bf16[128,2048]{1,0:T(8,128)(2,1)} fusion(f32[128,2048]{1,0:T(8,128)} %convolution_add_fusion.1, bf16[704,2048]{1,0:T(8,128)(2,1)S(1)} %copy-done, bf16[128,2048]{1,0:T(8,128)(2,1)S(1)} %reshape.262, bf16[2048,704]{0,1:T(8,128)(2,1)} %param.32, f32[128,704]{0,1:T(8,128)} %fusion.63), kind=kOutput, calls=%fused_computation.12 | convolution fusion | flops 739262464 | bytes 8224768 | tf_op jit(solution)/shard_map/dot_general | solution.py:150
  253.2 18.3 %reduce-scatter.2.cloned.1.call-done = bf16[128,512]{1,0:T(8,128)(2,1)} async-done(((bf16[128,2048]{1,0:T(8,128)(2,1)}), bf16[128,512]{1,0:T(8,128)(2,1)}) %reduce-scatter.2.cloned.1.call-update) | async-done | bytes 131088 | tf_op jit(solution)/shard_map/reduce_scatter | solution.py:151
  271.5 1.6 reshape.268
  (71 shorter events, 14.5 us)
Async XLA Ops:
  7.2 239.2 %copy-start = (bf16[704,2048]{1,0:T(8,128)(2,1)S(1)}, bf16[704,2048]{1,0:T(8,128)(2,1)}, u32[]{:S(2)}) copy-start(bf16[704,2048]{1,0:T(8,128)(2,1)} %param.33) | copy-start | bytes 8650756
  7.2 15.3 %copy-start.10 = (s32[64,2,6]{0,1,2:T(2,128)S(1)}, s32[64,2,6]{0,1,2:T(2,128)}, u32[]{:S(2)}) copy-start(s32[64,2,6]{0,1,2:T(2,128)} %param.26) | copy-start | bytes 9220
  7.2 63.7 %copy-start.12 = (s32[2]{0:T(128)S(1)}, s32[2]{0:T(128)}, u32[]{:S(2)}) copy-start(s32[2]{0:T(128)} %param.22) | copy-start | bytes 28
  7.2 102.5 %all-gather.2.cloned.1.call-start = ((), (), s32[]{:S(2)}) async-start(), calls=%async_computation.3 | async-start | bytes 3538944 | tf_op jit(solution)/shard_map/all_gather | solution.py:75
  9.7 152.2 %all-reduce.2.cloned.1.call-start = ((), (), s32[]{:S(2)}) async-start(), calls=%async_computation.4 | async-start | bytes 1048576 | tf_op jit(solution)/shard_map/psum | solution.py:98
  12.2 10.4 %collective-permute-start = (bf16[192,2,512]{0,2,1:T(8,128)(2,1)S(1)}, bf16[192,2,512]{0,2,1:T(8,128)(2,1)}, u32[]{:S(2)}, u32[]{:S(2)}) collective-permute-start(bf16[192,2,512]{0,2,1:T(8,128)(2,1)S(1)} %pad_maximum_fusion), channel_id=1, source_target_pairs={{0,4},{4,8},{8,12},{12,16},{16,20},{20,24},{24,28},{28,0},{1,5},{5... | collective-permute-start | bytes 1179656 | tf_op jit(solution)/shard_map/ppermute | solution.py:24
  22.5 11.1 %collective-permute-start.1 = (bf16[192,2,512]{0,2,1:T(8,128)(2,1)}, bf16[192,2,512]{0,2,1:T(8,128)(2,1)}, u32[]{:S(2)}, u32[]{:S(2)}) collective-permute-start(bf16[192,2,512]{0,2,1:T(8,128)(2,1)} %collective-permute-done), channel_id=1, source_target_pairs={{0,4},{4,8},{8,12},{12,16},{16,20},{20,24},{24,28},{28,0},{1,5},{5... | collective-permute-start | bytes 1179656 | tf_op jit(solution)/shard_map/ppermute | solution.py:24
  33.6 16.8 %collective-permute-start.2 = (bf16[192,2,512]{0,2,1:T(8,128)(2,1)}, bf16[192,2,512]{0,2,1:T(8,128)(2,1)}, u32[]{:S(2)}, u32[]{:S(2)}) collective-permute-start(bf16[192,2,512]{0,2,1:T(8,128)(2,1)} %collective-permute-done.1), channel_id=1, source_target_pairs={{0,4},{4,8},{8,12},{12,16},{16,20},{20,24},{24,28},{28,0},{1,5},{5... | collective-permute-start | bytes 1179656 | tf_op jit(solution)/shard_map/ppermute | solution.py:24
  50.5 9.8 %collective-permute-start.3 = (bf16[192,2,512]{0,2,1:T(8,128)(2,1)}, bf16[192,2,512]{0,2,1:T(8,128)(2,1)}, u32[]{:S(2)}, u32[]{:S(2)}) collective-permute-start(bf16[192,2,512]{0,2,1:T(8,128)(2,1)} %collective-permute-done.2), channel_id=1, source_target_pairs={{0,4},{4,8},{8,12},{12,16},{16,20},{20,24},{24,28},{28,0},{1,5},{5... | collective-permute-start | bytes 1179656 | tf_op jit(solution)/shard_map/ppermute | solution.py:24
  60.3 9.7 %collective-permute-start.4 = (bf16[192,2,512]{0,2,1:T(8,128)(2,1)}, bf16[192,2,512]{0,2,1:T(8,128)(2,1)S(1)}, u32[]{:S(2)}, u32[]{:S(2)}) collective-permute-start(bf16[192,2,512]{0,2,1:T(8,128)(2,1)} %collective-permute-done.3), channel_id=1, source_target_pairs={{0,4},{4,8},{8,12},{12,16},{16,20},{20,24},{24,28},{28,0},{1,5},{5... | collective-permute-start | bytes 1179656 | tf_op jit(solution)/shard_map/ppermute | solution.py:24
  70.0 0.8 copy-start.3
  70.8 9.5 %collective-permute-start.5 = (bf16[192,2,512]{0,2,1:T(8,128)(2,1)S(1)}, bf16[192,2,512]{0,2,1:T(8,128)(2,1)S(1)}, u32[]{:S(2)}, u32[]{:S(2)}) collective-permute-start(bf16[192,2,512]{0,2,1:T(8,128)(2,1)S(1)} %collective-permute-done.4), channel_id=1, source_target_pairs={{0,4},{4,8},{8,12},{12,16},{16,20},{20,24},{24,28},{28,0},{1,5},{5... | collective-permute-start | bytes 1179656 | tf_op jit(solution)/shard_map/ppermute | solution.py:24
  80.3 0.8 copy-start.4
  81.2 9.6 %collective-permute-start.6 = (bf16[192,2,512]{0,2,1:T(8,128)(2,1)S(1)}, bf16[192,2,512]{0,2,1:T(8,128)(2,1)}, u32[]{:S(2)}, u32[]{:S(2)}) collective-permute-start(bf16[192,2,512]{0,2,1:T(8,128)(2,1)S(1)} %collective-permute-done.5), channel_id=1, source_target_pairs={{0,4},{4,8},{8,12},{12,16},{16,20},{20,24},{24,28},{28,0},{1,5},{5... | collective-permute-start | bytes 1179656 | tf_op jit(solution)/shard_map/ppermute | solution.py:24
  102.6 3.6 %copy-start.5 = (pred[2,64,1536]{2,1,0:T(8,128)(4,1)S(1)}, pred[2,64,1536]{2,1,0:T(8,128)(4,1)}, u32[]{:S(2)}) copy-start(pred[2,64,1536]{2,1,0:T(8,128)(4,1)} %broadcast_or_fusion) | copy-start | bytes 589828
  102.6 3.6 %copy-start.8 = (bf16[64,2,4,128]{3,2,1,0:T(4,128)(2,1)S(1)}, bf16[64,2,4,128]{3,2,1,0:T(4,128)(2,1)}, u32[]{:S(2)}) copy-start(bf16[64,2,4,128]{3,2,1,0:T(4,128)(2,1)} %reshape.257) | copy-start | bytes 393220
  107.2 1.7 copy-start.1
  118.4 6.3 %copy-start.11 = (f32[64,2,6]{0,1,2:T(2,128)S(1)}, f32[64,2,6]{0,1,2:T(2,128)}, u32[]{:S(2)}) copy-start(f32[64,2,6]{0,1,2:T(2,128)} %param.27) | copy-start | bytes 9220
  124.3 40.0 %copy-start.9 = (f32[2048]{0:T(1024)S(1)}, f32[2048]{0:T(1024)}, u32[]{:S(2)}) copy-start(f32[2048]{0:T(1024)} %param.25) | copy-start | bytes 24580
  163.4 0.8 copy-start.2
  192.0 8.5 %copy-start.7 = (bf16[8,2,24,2048]{3,2,1,0:T(8,128)(2,1)}, bf16[8,2,24,2048]{3,2,1,0:T(8,128)(2,1)S(1)}, u32[]{:S(2)}) copy-start(bf16[8,2,24,2048]{3,2,1,0:T(8,128)(2,1)S(1)} %all_to_all.10) | copy-start | bytes 4718596
  216.2 25.3 %all-to-all-start.1 = ((bf16[8,2,24,2048]{3,2,1,0:T(8,128)(2,1)}), bf16[8,2,24,2048]{3,2,1,0:T(8,128)(2,1)}, u32[]{:S(2)}, u32[]{:S(2)}) async-start(bf16[8,2,24,2048]{3,2,1,0:T(8,128)(2,1)} %copy.102), calls=%async_computation.1 | async-start | bytes 3145728 | tf_op jit(solution)/shard_map/all_to_all | solution.py:141
  220.5 51.0 %reduce-scatter.2.cloned.1.call-start = ((), (), s32[]{:S(2)}) async-start(), calls=%async_computation.5 | async-start | bytes 655360 | tf_op jit(solution)/shard_map/reduce_scatter | solution.py:151
  241.5 2.0 copy-start.6
Sparse Core Ops, SparseCore 0:
  9.9 38.6 all-gather.1
  124.4 37.4 all-reduce.1
  251.6 19.8 reduce-scatter.1
